TPU v7x, 256 devices: a whole 4x4x8 slice. The times are simulated.
256 devices in a mesh: dp: 16 (over z_lo, x), block: 16 (over z_hi, y, core).
Axes of the slice: x: 4, y: 4, z: 8 (z_hi: 2, z_lo: 4; z = z_hi * 4 + z_lo), core: 2. Of those that a mesh axis runs over, the one named last changes fastest.
Arguments:
- inputs: bfloat16 [6144, 8192], P('dp', 'block'), may hold values from -6 to 6
- weight_in: bfloat16 [512, 5, 16384], P('dp', None, 'block'), may hold values from -0.125 to 0.125
- weight_out: bfloat16 [1024, 5, 8192], P('dp', None, 'block'), may hold values from -0.078125 to 0.078125
- cotangent: bfloat16 [6144, 8192], P('dp', 'block'), may hold values from -6 to 6
Outputs:
- outputs: bfloat16 [6144, 8192], P('dp', 'block')
- input_grad: bfloat16 [6144, 8192], P('dp', 'block')
- grad_in: float32 [512, 5, 16384], P('dp', None, 'block')
- grad_out: float32 [1024, 5, 8192], P('dp', None, 'block')
All inputs are finite; a program needn't handle non-finite values.
Results may differ from a plain program's by a relative error of at most 0.017.
Values may be sent and summed in bfloat16 or wider, within the bound.
No kernel may reach another device: no remote copies, remote signals or barrier semaphores. Data moves between devices by JAX's collectives and lax.ppermute only.
A program may use at most 128 MiB of HBM per device.

v0:
```python
import jax
import jax.numpy as jnp
from jax import lax
from jax.sharding import PartitionSpec as P


def swapped(value, axis, distance):
    mask = 2**distance
    pairs = [(source, source ^ mask) for source in range(lax.axis_size(axis))]
    return lax.ppermute(value, axis, pairs)


def gelu_tanh(value):
    return jax.nn.gelu(value, approximate=True)


def rounded(value):
    return lax.optimization_barrier(value.astype(jnp.bfloat16)).astype(jnp.float32)


def reduce_in(in_stack, pre_grad, shard_rows):

    def term(start, count):
        return jnp.einsum("tkc,th->ckh", in_stack, pre_grad, preferred_element_type=jnp.float32)

    return lax.psum_scatter(
        term(jnp.int32(0), lax.axis_size("dp") * shard_rows).astype(jnp.bfloat16),
        "dp",
        scatter_dimension=0,
        tiled=True,
    ).astype(jnp.float32)


def reduce_out(hid_stack, cotangent, shard_rows):

    def term(start, count):
        return jnp.einsum("tkh,tc->hkc", hid_stack, cotangent, preferred_element_type=jnp.float32)

    return lax.psum_scatter(
        term(jnp.int32(0), lax.axis_size("dp") * shard_rows).astype(jnp.bfloat16),
        "dp",
        scatter_dimension=0,
        tiled=True,
    ).astype(jnp.float32)


def body(inputs, weight_in, weight_out, cotangent):
    levels = lax.axis_size("block").bit_length() - 1
    weight_in_all, weight_out_all = (
        lax.all_gather(weight_in, "dp", axis=0, tiled=True),
        lax.all_gather(weight_out, "dp", axis=0, tiled=True),
    )
    pieces = [inputs]
    for level_bit in range(levels):
        pieces.append(swapped(inputs, "block", level_bit))
    in_stack = jnp.stack(pieces, axis=1)
    pre_act = jnp.einsum("tkc,ckh->th", in_stack, weight_in_all, preferred_element_type=jnp.float32)
    hidden = gelu_tanh(pre_act).astype(jnp.bfloat16)
    hid_pieces = [hidden]
    for level_bit in range(levels):
        hid_pieces.append(swapped(hidden, "block", level_bit))
    hid_stack = jnp.stack(hid_pieces, axis=1)
    outputs = jnp.einsum(
        "tkh,hkc->tc", hid_stack, weight_out_all, preferred_element_type=jnp.float32
    ).astype(jnp.bfloat16)
    back_terms = jnp.einsum(
        "tc,hkc->tkh", cotangent, weight_out_all, preferred_element_type=jnp.float32
    )
    back_round = back_terms.astype(jnp.bfloat16)
    hid_grad = rounded(back_terms[:, 0, :])
    for level_bit in range(levels):
        arrived = swapped(back_round[:, level_bit + 1, :], "block", level_bit)
        hid_grad = hid_grad + arrived.astype(jnp.float32)
    slope = jax.vjp(gelu_tanh, pre_act)[1](hid_grad)[0]
    pre_grad = slope.astype(jnp.bfloat16)
    in_terms = jnp.einsum(
        "th,ckh->tkc", pre_grad, weight_in_all, preferred_element_type=jnp.float32
    )
    in_round = in_terms.astype(jnp.bfloat16)
    in_total = rounded(in_terms[:, 0, :])
    for level_bit in range(levels):
        arrived = swapped(in_round[:, level_bit + 1, :], "block", level_bit)
        in_total = in_total + arrived.astype(jnp.float32)
    input_grad = in_total.astype(jnp.bfloat16)
    grad_in = reduce_in(in_stack, pre_grad, weight_in.shape[0])
    grad_out = reduce_out(hid_stack, cotangent, weight_out.shape[0])
    return (outputs, input_grad, grad_in, grad_out)


def solution(mesh):
    placed = (P("dp", "block"), P("dp", None, "block"), P("dp", None, "block"), P("dp", "block"))
    return jax.shard_map(
        body,
        mesh=mesh,
        in_specs=placed,
        out_specs=(
            P("dp", "block"),
            P("dp", "block"),
            P("dp", None, "block"),
            P("dp", None, "block"),
        ),
        check_vma=False,
    )
```

profile of v0, /device:TPU:8, one launch (start us, length us, event | category | flops | bytes accessed | tf_op | source)
XLA Modules:
  0.0 489.9 jit_solution(4013147169355985098)
XLA Ops:
  7.2 0.7 all-gather.5.cloned.1.call-update
  8.0 0.7 all-gather.3.cloned.1.call-update
  8.7 0.1 collective-permute-start
  8.8 2.2 collective-permute-start.1
  11.1 0.9 collective-permute-start.2
  11.9 7.2 %collective-permute-start.3 = (bf16[384,512]{1,0:T(8,128)(2,1)}, bf16[384,512]{1,0:T(8,128)(2,1)}, u32[]{:S(2)}, u32[]{:S(2)}) collective-permute-start(bf16[384,512]{1,0:T(8,128)(2,1)} %param.4), channel_id=1, source_target_pairs={{0,8},{1,9},{2,10},{3,11},{4,12},{5,13},{6,14},{7,15},{8,0},{9,1},... | collective-permute-start | bytes 1179656 | tf_op jit(solution)/shard_map/ppermute | solution.py:10
  19.1 1.8 bitcast_dynamic-update-slice_fusion.9
  20.9 0.8 bitcast_dynamic-update-slice_fusion.8
  21.7 0.8 bitcast_dynamic-update-slice_fusion.7
  22.5 7.5 %collective-permute-done.2 = bf16[384,512]{1,0:T(8,128)(2,1)S(1)} collective-permute-done((bf16[384,512]{1,0:T(8,128)(2,1)}, bf16[384,512]{1,0:T(8,128)(2,1)S(1)}, u32[]{:S(2)}, u32[]{:S(2)}) %collective-permute-start.2) | collective-permute-done | bytes 393248 | tf_op jit(solution)/shard_map/ppermute | solution.py:10
  30.0 0.8 bitcast_dynamic-update-slice_fusion.6
  30.8 80.7 %all-gather.5.cloned.1.call-done = bf16[1024,5,512]{2,0,1:T(8,128)(2,1)} async-done(((bf16[64,5,512]{2,0,1:T(8,128)(2,1)}), bf16[1024,5,512]{2,0,1:T(8,128)(2,1)}) %all-gather.5.cloned.1.call-update) | async-done | bytes 5242896 | tf_op jit(solution)/shard_map/all_gather | solution.py:51
  111.4 4.7 convert_bitcast_fusion.2
  116.2 1.8 slice_bitcast_fusion.4
  117.9 3.5 collective-permute-start.11
  121.4 2.3 collective-permute-start.10
  123.7 2.5 collective-permute-start.9
  126.2 1.8 bitcast_dynamic-update-slice_fusion.5
  128.0 83.3 %all-gather.3.cloned.1.call-done = bf16[512,5,1024]{2,0,1:T(8,128)(2,1)} async-done(((bf16[32,5,1024]{2,0,1:T(8,128)(2,1)}), bf16[512,5,1024]{2,0,1:T(8,128)(2,1)}) %all-gather.3.cloned.1.call-update) | async-done | bytes 5242896 | tf_op jit(solution)/shard_map/all_gather | solution.py:50
  211.3 6.8 %bitcast_dynamic-update-slice_fusion.4 = (bf16[384,5,1024]{2,0,1:T(8,128)(2,1)}, bf16[384,1024]{1,0:T(8,128)(2,1)}, f32[384,1024,1]{1,0,2:T(8,128)S(1)}) fusion(bf16[384,5,512]{2,0,1:T(8,128)(2,1)} %bitcast_dynamic-update-slice_fusion.5, bf16[512,5,1024]{2,0,1:T(8,128)(2,1)} %all-gather.3.cloned.1.call-done), kind=kOutput, calls=%fused_computation.31 | convolution fusion | flops 2016804864 | bytes 10354688 | tf_op jit(solution)/shard_map/tkc,ckh->th/dot_general | solution.py:57
  218.1 0.9 copy-done.1
  219.0 2.9 fusion.6
  221.9 6.2 %convert_bitcast_fusion.1 = bf16[512,5,1024]{0,2,1:T(8,128)(2,1)} fusion(bf16[384,5,512]{2,0,1:T(8,128)(2,1)} %bitcast_dynamic-update-slice_fusion.5, bf16[384,1024]{1,0:T(8,128)(2,1)S(1)} %fusion.6), kind=kOutput, calls=%fused_computation.1 | convolution fusion | flops 2015887360 | bytes 7995392 | tf_op jit(solution)/shard_map/tkc,th->ckh/dot_general | solution.py:24
  228.1 11.9 %copy.14 = bf16[512,5,1024]{2,1,0:T(8,128)(2,1)} copy(bf16[512,5,1024]{0,2,1:T(8,128)(2,1)} %convert_bitcast_fusion.1) | data formatting | bytes 10485760 | tf_op jit(solution)/shard_map/convert_element_type | solution.py:27
  240.1 1.1 copy-done.3
  241.2 1.1 collective-permute-start.5
  242.2 0.8 collective-permute-start.6
  243.0 3.8 collective-permute-start.7
  246.8 1.0 bitcast_dynamic-update-slice_fusion.3
  247.8 13.8 %collective-permute-done.5 = bf16[384,1024]{1,0:T(8,128)(2,1)S(1)} collective-permute-done((bf16[384,1024]{1,0:T(8,128)(2,1)S(1)}, bf16[384,1024]{1,0:T(8,128)(2,1)S(1)}, u32[]{:S(2)}, u32[]{:S(2)}) %collective-permute-start.5) | collective-permute-done | bytes 786464 | tf_op jit(solution)/shard_map/ppermute | solution.py:10
  261.6 0.9 bitcast_dynamic-update-slice_fusion.2
  262.5 15.2 %collective-permute-done.6 = bf16[384,1024]{1,0:T(8,128)(2,1)S(1)} collective-permute-done((bf16[384,1024]{1,0:T(8,128)(2,1)S(1)}, bf16[384,1024]{1,0:T(8,128)(2,1)S(1)}, u32[]{:S(2)}, u32[]{:S(2)}) %collective-permute-start.6) | collective-permute-done | bytes 786464 | tf_op jit(solution)/shard_map/ppermute | solution.py:10
  277.8 1.0 bitcast_dynamic-update-slice_fusion.1
  278.7 16.0 %collective-permute-done.7 = bf16[384,1024]{1,0:T(8,128)(2,1)S(1)} collective-permute-done((bf16[384,1024]{1,0:T(8,128)(2,1)S(1)}, bf16[384,1024]{1,0:T(8,128)(2,1)S(1)}, u32[]{:S(2)}, u32[]{:S(2)}) %collective-permute-start.7) | collective-permute-done | bytes 786464 | tf_op jit(solution)/shard_map/ppermute | solution.py:10
  294.7 0.9 bitcast_dynamic-update-slice_fusion
  295.7 6.8 %convert_bitcast_fusion = bf16[1024,5,512]{2,0,1:T(8,128)(2,1)} fusion(bf16[384,5,1024]{2,0,1:T(8,128)(2,1)} %bitcast_dynamic-update-slice_fusion, bf16[384,512]{1,0:T(8,128)(2,1)S(1)} %copy-done), kind=kOutput, calls=%fused_computation | convolution fusion | flops 2015887360 | bytes 9568256 | tf_op jit(solution)/shard_map/tkh,tc->hkc/dot_general | solution.py:37
  302.5 4.8 convert_bitcast_fusion.3
  307.3 0.2 slice_bitcast_fusion.9
  307.5 4.8 collective-permute-start.15
  312.3 2.5 collective-permute-start.14
  314.9 0.3 collective-permute-start.13
  315.1 5.5 %fusion.10 = bf16[384,512]{1,0:T(8,128)(2,1)} fusion(bf16[384,5,1024]{2,0,1:T(8,128)(2,1)S(1)} %copy-done.2, bf16[1024,5,512]{2,0,1:T(8,128)(2,1)} %all-gather.5.cloned.1.call-done), kind=kOutput, calls=%fused_computation.19 | convolution fusion | flops 2013462528 | bytes 9568256 | tf_op jit(solution)/shard_map/tkh,hkc->tc/dot_general | solution.py:63
  320.6 15.9 %collective-permute-done.15 = bf16[384,512]{1,0:T(8,128)(2,1)S(1)} collective-permute-done((bf16[384,512]{1,0:T(8,128)(2,1)S(1)}, bf16[384,512]{1,0:T(8,128)(2,1)S(1)}, u32[]{:S(2)}, u32[]{:S(2)}) %collective-permute-start.15) | collective-permute-done | bytes 393248 | tf_op jit(solution)/shard_map/ppermute | solution.py:10
  336.5 1.0 add_convert_fusion
  337.5 47.4 %reduce-scatter.3.cloned.1.call-done = bf16[32,5,1024]{2,1,0:T(8,128)(2,1)} async-done(((bf16[512,5,1024]{2,1,0:T(8,128)(2,1)}), bf16[32,5,1024]{2,1,0:T(8,128)(2,1)}) %reduce-scatter.3.cloned.1.call-update) | async-done | bytes 327696 | tf_op jit(solution)/shard_map/reduce_scatter | solution.py:26
  385.0 2.1 copy.16
  387.1 94.4 %reduce-scatter.5.cloned.1.call-done = bf16[64,5,512]{2,0,1:T(8,128)(2,1)} async-done(((bf16[1024,5,512]{2,0,1:T(8,128)(2,1)}), bf16[64,5,512]{2,0,1:T(8,128)(2,1)}) %reduce-scatter.5.cloned.1.call-update) | async-done | bytes 327696 | tf_op jit(solution)/shard_map/reduce_scatter | solution.py:39
  481.5 1.9 convert_element_type.91
  (26 shorter events, 0.2 us)
Async XLA Ops:
  7.2 104.3 %copy-start = (bf16[384,512]{1,0:T(8,128)(2,1)S(1)}, bf16[384,512]{1,0:T(8,128)(2,1)}, u32[]{:S(2)}) copy-start(bf16[384,512]{1,0:T(8,128)(2,1)} %param.7) | copy-start | bytes 1179652
  7.2 104.3 %all-gather.5.cloned.1.call-start = ((), (), s32[]{:S(2)}) async-start(), calls=%async_computation.3 | async-start | bytes 5570560 | tf_op jit(solution)/shard_map/all_gather | solution.py:51
  7.9 203.4 %all-gather.3.cloned.1.call-start = ((), (), s32[]{:S(2)}) async-start(), calls=%async_computation.2 | async-start | bytes 5570560 | tf_op jit(solution)/shard_map/all_gather | solution.py:50
  8.7 376.3 %reduce-scatter.3.cloned.1.call-start = ((), (), s32[]{:S(2)}) async-start(), calls=%async_computation.4 | async-start | bytes 8912896 | tf_op jit(solution)/shard_map/reduce_scatter | solution.py:26
  8.7 12.2 %collective-permute-start = (bf16[384,512]{1,0:T(8,128)(2,1)}, bf16[384,512]{1,0:T(8,128)(2,1)S(1)}, u32[]{:S(2)}, u32[]{:S(2)}) collective-permute-start(bf16[384,512]{1,0:T(8,128)(2,1)} %param.4), channel_id=1, source_target_pairs={{0,1},{1,0},{2,3},{3,2},{4,5},{5,4},{6,7},{7,6},{8,9},{9,8},{10,11... | collective-permute-start | bytes 1179656 | tf_op jit(solution)/shard_map/ppermute | solution.py:10
  8.8 12.9 %collective-permute-start.1 = (bf16[384,512]{1,0:T(8,128)(2,1)}, bf16[384,512]{1,0:T(8,128)(2,1)S(1)}, u32[]{:S(2)}, u32[]{:S(2)}) collective-permute-start(bf16[384,512]{1,0:T(8,128)(2,1)} %param.4), channel_id=1, source_target_pairs={{0,2},{1,3},{2,0},{3,1},{4,6},{5,7},{6,4},{7,5},{8,10},{9,11},{10,... | collective-permute-start | bytes 1179656 | tf_op jit(solution)/shard_map/ppermute | solution.py:10
  11.1 18.9 %collective-permute-start.2 = (bf16[384,512]{1,0:T(8,128)(2,1)}, bf16[384,512]{1,0:T(8,128)(2,1)S(1)}, u32[]{:S(2)}, u32[]{:S(2)}) collective-permute-start(bf16[384,512]{1,0:T(8,128)(2,1)} %param.4), channel_id=1, source_target_pairs={{0,4},{1,5},{2,6},{3,7},{4,0},{5,1},{6,2},{7,3},{8,12},{9,13},{10,... | collective-permute-start | bytes 1179656 | tf_op jit(solution)/shard_map/ppermute | solution.py:10
  11.9 114.3 %collective-permute-start.3 = (bf16[384,512]{1,0:T(8,128)(2,1)}, bf16[384,512]{1,0:T(8,128)(2,1)}, u32[]{:S(2)}, u32[]{:S(2)}) collective-permute-start(bf16[384,512]{1,0:T(8,128)(2,1)} %param.4), channel_id=1, source_target_pairs={{0,8},{1,9},{2,10},{3,11},{4,12},{5,13},{6,14},{7,15},{8,0},{9,1},... | collective-permute-start | bytes 1179656 | tf_op jit(solution)/shard_map/ppermute | solution.py:10
  117.9 100.2 %collective-permute-start.11 = (bf16[384,1024]{1,0:T(8,128)(2,1)}, bf16[384,1024]{1,0:T(8,128)(2,1)S(1)}, u32[]{:S(2)}, u32[]{:S(2)}) collective-permute-start(bf16[384,1024]{1,0:T(8,128)(2,1)} %get-tuple-element.15), channel_id=1, source_target_pairs={{0,8},{1,9},{2,10},{3,11},{4,12},{5,13},{6,14},{7,15},{8,0},{9,1},... | collective-permute-start | bytes 2359304 | tf_op jit(solution)/shard_map/ppermute | solution.py:10
  121.4 96.7 %collective-permute-start.10 = (bf16[384,1024]{1,0:T(8,128)(2,1)}, bf16[384,1024]{1,0:T(8,128)(2,1)S(1)}, u32[]{:S(2)}, u32[]{:S(2)}) collective-permute-start(bf16[384,1024]{1,0:T(8,128)(2,1)} %get-tuple-element.16), channel_id=1, source_target_pairs={{0,4},{1,5},{2,6},{3,7},{4,0},{5,1},{6,2},{7,3},{8,12},{9,13},{10,... | collective-permute-start | bytes 2359304 | tf_op jit(solution)/shard_map/ppermute | solution.py:10
  123.7 94.4 %collective-permute-start.9 = (bf16[384,1024]{1,0:T(8,128)(2,1)}, bf16[384,1024]{1,0:T(8,128)(2,1)S(1)}, u32[]{:S(2)}, u32[]{:S(2)}) collective-permute-start(bf16[384,1024]{1,0:T(8,128)(2,1)} %get-tuple-element.17), channel_id=1, source_target_pairs={{0,2},{1,3},{2,0},{3,1},{4,6},{5,7},{6,4},{7,5},{8,10},{9,11},{10,... | collective-permute-start | bytes 2359304 | tf_op jit(solution)/shard_map/ppermute | solution.py:10
  126.2 92.0 %collective-permute-start.8 = (bf16[384,1024]{1,0:T(8,128)(2,1)}, bf16[384,1024]{1,0:T(8,128)(2,1)}, u32[]{:S(2)}, u32[]{:S(2)}) collective-permute-start(bf16[384,1024]{1,0:T(8,128)(2,1)} %get-tuple-element.18), channel_id=1, source_target_pairs={{0,1},{1,0},{2,3},{3,2},{4,5},{5,4},{6,7},{7,6},{8,9},{9,8},{10,11... | collective-permute-start | bytes 2359304 | tf_op jit(solution)/shard_map/ppermute | solution.py:10
  218.1 0.9 copy-start.1
  240.0 1.1 copy-start.3
  240.1 241.4 %reduce-scatter.5.cloned.1.call-start = ((), (), s32[]{:S(2)}) async-start(), calls=%async_computation.5 | async-start | bytes 5570560 | tf_op jit(solution)/shard_map/reduce_scatter | solution.py:39
  241.2 5.6 %collective-permute-start.4 = (bf16[384,1024]{1,0:T(8,128)(2,1)S(1)}, bf16[384,1024]{1,0:T(8,128)(2,1)S(1)}, u32[]{:S(2)}, u32[]{:S(2)}) collective-permute-start(bf16[384,1024]{1,0:T(8,128)(2,1)S(1)} %copy-done.3), channel_id=1, source_target_pairs={{0,1},{1,0},{2,3},{3,2},{4,5},{5,4},{6,7},{7,6},{8,9},{9,8},{10,11... | collective-permute-start | bytes 2359304 | tf_op jit(solution)/shard_map/ppermute | solution.py:10
  241.2 20.4 %collective-permute-start.5 = (bf16[384,1024]{1,0:T(8,128)(2,1)S(1)}, bf16[384,1024]{1,0:T(8,128)(2,1)S(1)}, u32[]{:S(2)}, u32[]{:S(2)}) collective-permute-start(bf16[384,1024]{1,0:T(8,128)(2,1)S(1)} %copy-done.3), channel_id=1, source_target_pairs={{0,2},{1,3},{2,0},{3,1},{4,6},{5,7},{6,4},{7,5},{8,10},{9,11},{10,... | collective-permute-start | bytes 2359304 | tf_op jit(solution)/shard_map/ppermute | solution.py:10
  242.2 35.5 %collective-permute-start.6 = (bf16[384,1024]{1,0:T(8,128)(2,1)S(1)}, bf16[384,1024]{1,0:T(8,128)(2,1)S(1)}, u32[]{:S(2)}, u32[]{:S(2)}) collective-permute-start(bf16[384,1024]{1,0:T(8,128)(2,1)S(1)} %copy-done.3), channel_id=1, source_target_pairs={{0,4},{1,5},{2,6},{3,7},{4,0},{5,1},{6,2},{7,3},{8,12},{9,13},{10,... | collective-permute-start | bytes 2359304 | tf_op jit(solution)/shard_map/ppermute | solution.py:10
  243.0 51.7 %collective-permute-start.7 = (bf16[384,1024]{1,0:T(8,128)(2,1)S(1)}, bf16[384,1024]{1,0:T(8,128)(2,1)S(1)}, u32[]{:S(2)}, u32[]{:S(2)}) collective-permute-start(bf16[384,1024]{1,0:T(8,128)(2,1)S(1)} %copy-done.3), channel_id=1, source_target_pairs={{0,8},{1,9},{2,10},{3,11},{4,12},{5,13},{6,14},{7,15},{8,0},{9,1},... | collective-permute-start | bytes 2359304 | tf_op jit(solution)/shard_map/ppermute | solution.py:10
  307.3 7.8 %copy-start.2 = (bf16[384,5,1024]{2,0,1:T(8,128)(2,1)S(1)}, bf16[384,5,1024]{2,0,1:T(8,128)(2,1)}, u32[]{:S(2)}) copy-start(bf16[384,5,1024]{2,0,1:T(8,128)(2,1)} %bitcast_dynamic-update-slice_fusion) | copy-start | bytes 11796484
  307.5 29.0 %collective-permute-start.15 = (bf16[384,512]{1,0:T(8,128)(2,1)S(1)}, bf16[384,512]{1,0:T(8,128)(2,1)S(1)}, u32[]{:S(2)}, u32[]{:S(2)}) collective-permute-start(bf16[384,512]{1,0:T(8,128)(2,1)S(1)} %get-tuple-element.20), channel_id=1, source_target_pairs={{0,8},{1,9},{2,10},{3,11},{4,12},{5,13},{6,14},{7,15},{8,0},{9,1},... | collective-permute-start | bytes 1179656 | tf_op jit(solution)/shard_map/ppermute | solution.py:10
  312.3 24.2 %collective-permute-start.14 = (bf16[384,512]{1,0:T(8,128)(2,1)S(1)}, bf16[384,512]{1,0:T(8,128)(2,1)S(1)}, u32[]{:S(2)}, u32[]{:S(2)}) collective-permute-start(bf16[384,512]{1,0:T(8,128)(2,1)S(1)} %get-tuple-element.21), channel_id=1, source_target_pairs={{0,4},{1,5},{2,6},{3,7},{4,0},{5,1},{6,2},{7,3},{8,12},{9,13},{10,... | collective-permute-start | bytes 1179656 | tf_op jit(solution)/shard_map/ppermute | solution.py:10
  314.9 21.7 %collective-permute-start.13 = (bf16[384,512]{1,0:T(8,128)(2,1)S(1)}, bf16[384,512]{1,0:T(8,128)(2,1)S(1)}, u32[]{:S(2)}, u32[]{:S(2)}) collective-permute-start(bf16[384,512]{1,0:T(8,128)(2,1)S(1)} %get-tuple-element.22), channel_id=1, source_target_pairs={{0,2},{1,3},{2,0},{3,1},{4,6},{5,7},{6,4},{7,5},{8,10},{9,11},{10,... | collective-permute-start | bytes 1179656 | tf_op jit(solution)/shard_map/ppermute | solution.py:10
  315.1 21.4 %collective-permute-start.12 = (bf16[384,512]{1,0:T(8,128)(2,1)S(1)}, bf16[384,512]{1,0:T(8,128)(2,1)S(1)}, u32[]{:S(2)}, u32[]{:S(2)}) collective-permute-start(bf16[384,512]{1,0:T(8,128)(2,1)S(1)} %get-tuple-element.23), channel_id=1, source_target_pairs={{0,1},{1,0},{2,3},{3,2},{4,5},{5,4},{6,7},{7,6},{8,9},{9,8},{10,11... | collective-permute-start | bytes 1179656 | tf_op jit(solution)/shard_map/ppermute | solution.py:10
Sparse Core Ops, SparseCore 0:
  9.8 101.6 all-gather.4
  113.2 98.0 all-gather.2
  240.2 144.7 reduce-scatter.2
  387.4 94.0 reduce-scatter.4
where the time goes:
time: 491 us; the launch traced here: 490 us
  waiting for transfers between devices  376 us (77%)
  matrix products  34.8 us (7%)
  starting transfers between devices  32 us (7%)
  local copies, waits for them, and re-layouts  27.7 us (6%)
  between operations  13.9 us (3%)
  other arithmetic  5.79 us (1%)
    reduce_scatter x1, waiting for transfers between devices, reduce_out(): lax.psum_scatter(term(jnp.int32(0), lax.axis_size('dp') * shard_rows).ast...  94.4 us
    all_gather x1, waiting for transfers between devices, body(): lax.all_gather(weight_in, 'dp', axis=0, tiled=True)  83.3 us
    all_gather x1, waiting for transfers between devices, body(): lax.all_gather(weight_out, 'dp', axis=0, tiled=True)  80.7 us
    ppermute x16, waiting for transfers between devices, swapped(): return lax.ppermute(value, axis, pairs)  68.5 us
    reduce_scatter x1, waiting for transfers between devices, reduce_in(): lax.psum_scatter(term(jnp.int32(0), lax.axis_size('dp') * shard_rows).ast...  47.4 us
    ppermute x16, starting transfers between devices, swapped(): return lax.ppermute(value, axis, pairs)  31.9 us
    convert_element_type x1, local copies, waits for them, and re-layouts, reduce_in(): term(jnp.int32(0), lax.axis_size('dp') * shard_rows).astype(jnp.bfloat16)  11.9 us
    unnamed x16, local copies, waits for them, and re-layouts  11.1 us
  transfers between devices with their start and end apart: 20, of which 9 were waited for; matrix products, arithmetic and copies ran while one was open for 9% of the time, Pallas kernels for 0%

commit v1 on v0

--- a/solution.py
+++ b/solution.py
@@ -47,7 +47,9 @@
 def body(inputs, weight_in, weight_out, cotangent):
     levels = lax.axis_size("block").bit_length() - 1
     weight_in_all, weight_out_all = (
-        lax.all_gather(weight_in, "dp", axis=0, tiled=True),
+        jnp.concatenate(
+            lax.all_to_all(jnp.stack([weight_in] * lax.axis_size("dp")), "dp", 0, 0), axis=0
+        ),
         lax.all_gather(weight_out, "dp", axis=0, tiled=True),
     )
     pieces = [inputs]

time: 491 us -> 549 us (1.12)
  waiting for transfers between devices: 376 us -> 426 us
  local copies, waits for them, and re-layouts: 27.7 us -> 34.9 us
    all_gather x1 -> x0, waiting for transfers between devices: 83.3 us -> none  [body(): lax.all_gather(weight_in, 'dp', axis=0, tiled=True)]
    all_gather x1, waiting for transfers between devices: 80.7 us -> 146 us  [body(): lax.all_gather(weight_out, 'dp', axis=0, tiled=True)]
    reduce_scatter x1, waiting for transfers between devices: 47.4 us -> 110 us  [reduce_in(): lax.psum_scatter(term(jnp.int32(0), lax.axis_size('dp') * shard_rows).ast...]
    all_to_all x0 -> x1, starting transfers between devices: none -> 8.51 us  [body(): lax.all_to_all(jnp.stack([weight_in] * lax.axis_size('dp')), 'dp', 0, 0)]
    ppermute x16, starting transfers between devices: 31.9 us -> 23.7 us  [swapped(): return lax.ppermute(value, axis, pairs)]
    unnamed x16 -> x18, local copies, waits for them, and re-layouts: 11.1 us -> 11.2 us
  transfers between devices with their start and end apart: 20 -> 20, of which waited for: 9 -> 12; matrix products, arithmetic and copies ran while one was open for 9% -> 9% of each run, Pallas kernels for 0% -> 0%
where the time goes in v1:
time: 549 us; the launch traced here: 548 us
  waiting for transfers between devices  426 us (78%)
  local copies, waits for them, and re-layouts  34.9 us (6%)
  matrix products  34.6 us (6%)
  starting transfers between devices  32.4 us (6%)
  between operations  13.8 us (3%)
  other arithmetic  5.79 us (1%)
    all_gather x1, waiting for transfers between devices, body(): lax.all_gather(weight_out, 'dp', axis=0, tiled=True)  146 us
    reduce_scatter x1, waiting for transfers between devices, reduce_in(): lax.psum_scatter(term(jnp.int32(0), lax.axis_size('dp') * shard_rows).ast...  110 us
    reduce_scatter x1, waiting for transfers between devices, reduce_out(): lax.psum_scatter(term(jnp.int32(0), lax.axis_size('dp') * shard_rows).ast...  96.5 us
    ppermute x16, waiting for transfers between devices, swapped(): return lax.ppermute(value, axis, pairs)  73.5 us
    ppermute x16, starting transfers between devices, swapped(): return lax.ppermute(value, axis, pairs)  23.7 us
    convert_element_type x1, local copies, waits for them, and re-layouts, reduce_in(): term(jnp.int32(0), lax.axis_size('dp') * shard_rows).astype(jnp.bfloat16)  11.9 us
    unnamed x18, local copies, waits for them, and re-layouts  11.2 us
  transfers between devices with their start and end apart: 20, of which 12 were waited for; matrix products, arithmetic and copies ran while one was open for 9% of the time, Pallas kernels for 0%

profile of v1, /device:TPU:8, one launch (start us, length us, event | category | flops | bytes accessed | tf_op | source)
XLA Modules:
  0.0 547.8 jit_solution(13107108790677977177)
XLA Ops:
  7.2 0.7 all-gather.2.cloned.1.call-update
  7.9 3.9 stack.61
  11.8 8.5 %all-to-all-start = ((bf16[16,32,5,1024]{3,1,2,0:T(8,128)(2,1)}), bf16[16,32,5,1024]{3,1,2,0:T(8,128)(2,1)}, u32[]{:S(2)}, u32[]{:S(2)}) async-start(bf16[16,32,5,1024]{3,1,2,0:T(8,128)(2,1)} %stack.61), calls=%async_computation | async-start | bytes 10485760 | tf_op jit(solution)/shard_map/all_to_all | solution.py:51
  21.0 2.6 collective-permute-start.2
  23.6 4.5 collective-permute-start.3
  28.1 1.8 bitcast_dynamic-update-slice_fusion.9
  29.9 0.8 bitcast_dynamic-update-slice_fusion.8
  30.7 2.1 collective-permute-done.1
  32.8 0.8 bitcast_dynamic-update-slice_fusion.7
  33.6 8.1 %collective-permute-done.2 = bf16[384,512]{1,0:T(8,128)(2,1)S(1)} collective-permute-done((bf16[384,512]{1,0:T(8,128)(2,1)}, bf16[384,512]{1,0:T(8,128)(2,1)S(1)}, u32[]{:S(2)}, u32[]{:S(2)}) %collective-permute-start.2) | collective-permute-done | bytes 393248 | tf_op jit(solution)/shard_map/ppermute | solution.py:10
  41.7 0.8 bitcast_dynamic-update-slice_fusion.6
  42.4 146.0 %all-gather.2.cloned.1.call-done = bf16[1024,5,512]{2,0,1:T(8,128)(2,1)} async-done(((bf16[64,5,512]{2,0,1:T(8,128)(2,1)}), bf16[1024,5,512]{2,0,1:T(8,128)(2,1)}) %all-gather.2.cloned.1.call-update) | async-done | bytes 5242896 | tf_op jit(solution)/shard_map/all_gather | solution.py:53
  188.5 4.7 convert_bitcast_fusion.2
  193.2 1.8 slice_bitcast_fusion.4
  195.0 6.0 %collective-permute-start.11 = (bf16[384,1024]{1,0:T(8,128)(2,1)}, bf16[384,1024]{1,0:T(8,128)(2,1)S(1)}, u32[]{:S(2)}, u32[]{:S(2)}) collective-permute-start(bf16[384,1024]{1,0:T(8,128)(2,1)} %get-tuple-element.15), channel_id=1, source_target_pairs={{0,8},{1,9},{2,10},{3,11},{4,12},{5,13},{6,14},{7,15},{8,0},{9,1},... | collective-permute-start | bytes 2359304 | tf_op jit(solution)/shard_map/ppermute | solution.py:10
  201.1 2.3 collective-permute-start.10
  203.4 1.3 collective-permute-start.9
  204.6 1.8 bitcast_dynamic-update-slice_fusion.5
  206.4 3.1 copy.12
  209.6 6.7 %bitcast_dynamic-update-slice_fusion.4 = (bf16[384,5,1024]{2,0,1:T(8,128)(2,1)}, bf16[384,1024]{1,0:T(8,128)(2,1)}, f32[384,1024,1]{1,0,2:T(8,128)S(1)}) fusion(bf16[384,5,512]{2,0,1:T(8,128)(2,1)} %bitcast_dynamic-update-slice_fusion.5, bf16[512,5,1024]{2,0,1:T(8,128)(2,1)S(1)} %bitcast.90), kind=kOutput, calls=%fused_computation.31 | convolution fusion | flops 2016804864 | bytes 10354688 | tf_op jit(solution)/shard_map/tkc,ckh->th/dot_general | solution.py:59
  216.3 6.9 %collective-permute-done.10 = bf16[384,1024]{1,0:T(8,128)(2,1)S(1)} collective-permute-done((bf16[384,1024]{1,0:T(8,128)(2,1)}, bf16[384,1024]{1,0:T(8,128)(2,1)S(1)}, u32[]{:S(2)}, u32[]{:S(2)}) %collective-permute-start.10) | collective-permute-done | bytes 786464 | tf_op jit(solution)/shard_map/ppermute | solution.py:10
  223.2 12.4 %collective-permute-done.9 = bf16[384,1024]{1,0:T(8,128)(2,1)S(1)} collective-permute-done((bf16[384,1024]{1,0:T(8,128)(2,1)}, bf16[384,1024]{1,0:T(8,128)(2,1)S(1)}, u32[]{:S(2)}, u32[]{:S(2)}) %collective-permute-start.9) | collective-permute-done | bytes 786464 | tf_op jit(solution)/shard_map/ppermute | solution.py:10
  235.6 0.9 copy-done.2
  236.5 2.9 fusion.6
  239.4 6.2 %convert_bitcast_fusion.1 = bf16[512,5,1024]{0,2,1:T(8,128)(2,1)} fusion(bf16[384,5,512]{2,0,1:T(8,128)(2,1)} %bitcast_dynamic-update-slice_fusion.5, bf16[384,1024]{1,0:T(8,128)(2,1)S(1)} %fusion.6), kind=kOutput, calls=%fused_computation.1 | convolution fusion | flops 2015887360 | bytes 7995392 | tf_op jit(solution)/shard_map/tkc,th->ckh/dot_general | solution.py:24
  245.6 11.9 %copy.15 = bf16[512,5,1024]{2,1,0:T(8,128)(2,1)} copy(bf16[512,5,1024]{0,2,1:T(8,128)(2,1)} %convert_bitcast_fusion.1) | data formatting | bytes 10485760 | tf_op jit(solution)/shard_map/convert_element_type | solution.py:27
  257.6 1.1 copy-done.4
  258.7 0.7 collective-permute-start.5
  259.9 1.0 collective-permute-done.4
  260.9 1.0 bitcast_dynamic-update-slice_fusion.3
  262.0 17.1 %collective-permute-done.5 = bf16[384,1024]{1,0:T(8,128)(2,1)S(1)} collective-permute-done((bf16[384,1024]{1,0:T(8,128)(2,1)S(1)}, bf16[384,1024]{1,0:T(8,128)(2,1)S(1)}, u32[]{:S(2)}, u32[]{:S(2)}) %collective-permute-start.5) | collective-permute-done | bytes 786464 | tf_op jit(solution)/shard_map/ppermute | solution.py:10
  279.1 0.9 bitcast_dynamic-update-slice_fusion.2
  280.0 14.4 %collective-permute-done.6 = bf16[384,1024]{1,0:T(8,128)(2,1)S(1)} collective-permute-done((bf16[384,1024]{1,0:T(8,128)(2,1)S(1)}, bf16[384,1024]{1,0:T(8,128)(2,1)S(1)}, u32[]{:S(2)}, u32[]{:S(2)}) %collective-permute-start.6) | collective-permute-done | bytes 786464 | tf_op jit(solution)/shard_map/ppermute | solution.py:10
  294.4 1.0 bitcast_dynamic-update-slice_fusion.1
  295.4 0.9 bitcast_dynamic-update-slice_fusion
  296.4 6.8 %convert_bitcast_fusion = bf16[1024,5,512]{2,0,1:T(8,128)(2,1)} fusion(bf16[384,5,1024]{2,0,1:T(8,128)(2,1)} %bitcast_dynamic-update-slice_fusion, bf16[384,512]{1,0:T(8,128)(2,1)S(1)} %copy-done), kind=kOutput, calls=%fused_computation | convolution fusion | flops 2015887360 | bytes 9568256 | tf_op jit(solution)/shard_map/tkh,tc->hkc/dot_general | solution.py:37
  303.2 4.7 convert_bitcast_fusion.3
  308.1 0.6 collective-permute-start.15
  308.7 3.2 collective-permute-start.14
  311.9 1.3 collective-permute-start.13
  313.2 5.4 fusion.10
  318.7 4.7 collective-permute-done.15
  323.4 6.7 %collective-permute-done.13 = bf16[384,512]{1,0:T(8,128)(2,1)S(1)} collective-permute-done((bf16[384,512]{1,0:T(8,128)(2,1)S(1)}, bf16[384,512]{1,0:T(8,128)(2,1)S(1)}, u32[]{:S(2)}, u32[]{:S(2)}) %collective-permute-start.13) | collective-permute-done | bytes 393248 | tf_op jit(solution)/shard_map/ppermute | solution.py:10
  330.1 1.0 add_convert_fusion
  331.1 109.6 %reduce-scatter.3.cloned.1.call-done = bf16[32,5,1024]{2,1,0:T(8,128)(2,1)} async-done(((bf16[512,5,1024]{2,1,0:T(8,128)(2,1)}), bf16[32,5,1024]{2,1,0:T(8,128)(2,1)}) %reduce-scatter.3.cloned.1.call-update) | async-done | bytes 327696 | tf_op jit(solution)/shard_map/reduce_scatter | solution.py:26
  440.7 2.1 copy.17
  442.9 96.5 %reduce-scatter.5.cloned.1.call-done = bf16[64,5,512]{2,0,1:T(8,128)(2,1)} async-done(((bf16[1024,5,512]{2,0,1:T(8,128)(2,1)}), bf16[64,5,512]{2,0,1:T(8,128)(2,1)}) %reduce-scatter.5.cloned.1.call-update) | async-done | bytes 327696 | tf_op jit(solution)/shard_map/reduce_scatter | solution.py:39
  539.4 1.9 convert_element_type.91
  (29 shorter events, 1.6 us)
Async XLA Ops:
  7.2 181.3 %copy-start = (bf16[384,512]{1,0:T(8,128)(2,1)S(1)}, bf16[384,512]{1,0:T(8,128)(2,1)}, u32[]{:S(2)}) copy-start(bf16[384,512]{1,0:T(8,128)(2,1)} %param.7) | copy-start | bytes 1179652
  7.2 181.3 %all-gather.2.cloned.1.call-start = ((), (), s32[]{:S(2)}) async-start(), calls=%async_computation.3 | async-start | bytes 5570560 | tf_op jit(solution)/shard_map/all_gather | solution.py:53
  11.8 194.6 %all-to-all-start = ((bf16[16,32,5,1024]{3,1,2,0:T(8,128)(2,1)}), bf16[16,32,5,1024]{3,1,2,0:T(8,128)(2,1)}, u32[]{:S(2)}, u32[]{:S(2)}) async-start(bf16[16,32,5,1024]{3,1,2,0:T(8,128)(2,1)} %stack.61), calls=%async_computation | async-start | bytes 10485760 | tf_op jit(solution)/shard_map/all_to_all | solution.py:51
  20.3 420.4 %reduce-scatter.3.cloned.1.call-start = ((), (), s32[]{:S(2)}) async-start(), calls=%async_computation.4 | async-start | bytes 8912896 | tf_op jit(solution)/shard_map/reduce_scatter | solution.py:26
  20.4 9.5 %collective-permute-start = (bf16[384,512]{1,0:T(8,128)(2,1)}, bf16[384,512]{1,0:T(8,128)(2,1)S(1)}, u32[]{:S(2)}, u32[]{:S(2)}) collective-permute-start(bf16[384,512]{1,0:T(8,128)(2,1)} %param.4), channel_id=1, source_target_pairs={{0,1},{1,0},{2,3},{3,2},{4,5},{5,4},{6,7},{7,6},{8,9},{9,8},{10,11... | collective-permute-start | bytes 1179656 | tf_op jit(solution)/shard_map/ppermute | solution.py:10
  20.5 12.3 %collective-permute-start.1 = (bf16[384,512]{1,0:T(8,128)(2,1)}, bf16[384,512]{1,0:T(8,128)(2,1)S(1)}, u32[]{:S(2)}, u32[]{:S(2)}) collective-permute-start(bf16[384,512]{1,0:T(8,128)(2,1)} %param.4), channel_id=1, source_target_pairs={{0,2},{1,3},{2,0},{3,1},{4,6},{5,7},{6,4},{7,5},{8,10},{9,11},{10,... | collective-permute-start | bytes 1179656 | tf_op jit(solution)/shard_map/ppermute | solution.py:10
  21.0 20.6 %collective-permute-start.2 = (bf16[384,512]{1,0:T(8,128)(2,1)}, bf16[384,512]{1,0:T(8,128)(2,1)S(1)}, u32[]{:S(2)}, u32[]{:S(2)}) collective-permute-start(bf16[384,512]{1,0:T(8,128)(2,1)} %param.4), channel_id=1, source_target_pairs={{0,4},{1,5},{2,6},{3,7},{4,0},{5,1},{6,2},{7,3},{8,12},{9,13},{10,... | collective-permute-start | bytes 1179656 | tf_op jit(solution)/shard_map/ppermute | solution.py:10
  23.6 181.0 %collective-permute-start.3 = (bf16[384,512]{1,0:T(8,128)(2,1)}, bf16[384,512]{1,0:T(8,128)(2,1)}, u32[]{:S(2)}, u32[]{:S(2)}) collective-permute-start(bf16[384,512]{1,0:T(8,128)(2,1)} %param.4), channel_id=1, source_target_pairs={{0,8},{1,9},{2,10},{3,11},{4,12},{5,13},{6,14},{7,15},{8,0},{9,1},... | collective-permute-start | bytes 1179656 | tf_op jit(solution)/shard_map/ppermute | solution.py:10
  195.0 21.2 %collective-permute-start.11 = (bf16[384,1024]{1,0:T(8,128)(2,1)}, bf16[384,1024]{1,0:T(8,128)(2,1)S(1)}, u32[]{:S(2)}, u32[]{:S(2)}) collective-permute-start(bf16[384,1024]{1,0:T(8,128)(2,1)} %get-tuple-element.15), channel_id=1, source_target_pairs={{0,8},{1,9},{2,10},{3,11},{4,12},{5,13},{6,14},{7,15},{8,0},{9,1},... | collective-permute-start | bytes 2359304 | tf_op jit(solution)/shard_map/ppermute | solution.py:10
  201.1 22.1 %collective-permute-start.10 = (bf16[384,1024]{1,0:T(8,128)(2,1)}, bf16[384,1024]{1,0:T(8,128)(2,1)S(1)}, u32[]{:S(2)}, u32[]{:S(2)}) collective-permute-start(bf16[384,1024]{1,0:T(8,128)(2,1)} %get-tuple-element.16), channel_id=1, source_target_pairs={{0,4},{1,5},{2,6},{3,7},{4,0},{5,1},{6,2},{7,3},{8,12},{9,13},{10,... | collective-permute-start | bytes 2359304 | tf_op jit(solution)/shard_map/ppermute | solution.py:10
  203.4 32.2 %collective-permute-start.9 = (bf16[384,1024]{1,0:T(8,128)(2,1)}, bf16[384,1024]{1,0:T(8,128)(2,1)S(1)}, u32[]{:S(2)}, u32[]{:S(2)}) collective-permute-start(bf16[384,1024]{1,0:T(8,128)(2,1)} %get-tuple-element.17), channel_id=1, source_target_pairs={{0,2},{1,3},{2,0},{3,1},{4,6},{5,7},{6,4},{7,5},{8,10},{9,11},{10,... | collective-permute-start | bytes 2359304 | tf_op jit(solution)/shard_map/ppermute | solution.py:10
  204.6 31.0 %collective-permute-start.8 = (bf16[384,1024]{1,0:T(8,128)(2,1)}, bf16[384,1024]{1,0:T(8,128)(2,1)}, u32[]{:S(2)}, u32[]{:S(2)}) collective-permute-start(bf16[384,1024]{1,0:T(8,128)(2,1)} %get-tuple-element.18), channel_id=1, source_target_pairs={{0,1},{1,0},{2,3},{3,2},{4,5},{5,4},{6,7},{7,6},{8,9},{9,8},{10,11... | collective-permute-start | bytes 2359304 | tf_op jit(solution)/shard_map/ppermute | solution.py:10
  209.5 6.7 %copy-start.1 = (bf16[16,32,5,1024]{3,1,0,2:T(8,128)(2,1)}, bf16[16,32,5,1024]{3,1,0,2:T(8,128)(2,1)S(1)}, u32[]{:S(2)}) copy-start(bf16[16,32,5,1024]{3,1,0,2:T(8,128)(2,1)S(1)} %copy.12) | copy-start | bytes 15728644
  235.6 0.9 copy-start.2
  257.5 1.1 copy-start.4
  257.6 281.8 %reduce-scatter.5.cloned.1.call-start = ((), (), s32[]{:S(2)}) async-start(), calls=%async_computation.5 | async-start | bytes 5570560 | tf_op jit(solution)/shard_map/reduce_scatter | solution.py:39
  258.7 2.3 collective-permute-start.4
  258.7 20.4 %collective-permute-start.5 = (bf16[384,1024]{1,0:T(8,128)(2,1)S(1)}, bf16[384,1024]{1,0:T(8,128)(2,1)S(1)}, u32[]{:S(2)}, u32[]{:S(2)}) collective-permute-start(bf16[384,1024]{1,0:T(8,128)(2,1)S(1)} %copy-done.4), channel_id=1, source_target_pairs={{0,2},{1,3},{2,0},{3,1},{4,6},{5,7},{6,4},{7,5},{8,10},{9,11},{10,... | collective-permute-start | bytes 2359304 | tf_op jit(solution)/shard_map/ppermute | solution.py:10
  259.4 35.1 %collective-permute-start.6 = (bf16[384,1024]{1,0:T(8,128)(2,1)S(1)}, bf16[384,1024]{1,0:T(8,128)(2,1)S(1)}, u32[]{:S(2)}, u32[]{:S(2)}) collective-permute-start(bf16[384,1024]{1,0:T(8,128)(2,1)S(1)} %copy-done.4), channel_id=1, source_target_pairs={{0,4},{1,5},{2,6},{3,7},{4,0},{5,1},{6,2},{7,3},{8,12},{9,13},{10,... | collective-permute-start | bytes 2359304 | tf_op jit(solution)/shard_map/ppermute | solution.py:10
  259.7 35.7 %collective-permute-start.7 = (bf16[384,1024]{1,0:T(8,128)(2,1)S(1)}, bf16[384,1024]{1,0:T(8,128)(2,1)S(1)}, u32[]{:S(2)}, u32[]{:S(2)}) collective-permute-start(bf16[384,1024]{1,0:T(8,128)(2,1)S(1)} %copy-done.4), channel_id=1, source_target_pairs={{0,8},{1,9},{2,10},{3,11},{4,12},{5,13},{6,14},{7,15},{8,0},{9,1},... | collective-permute-start | bytes 2359304 | tf_op jit(solution)/shard_map/ppermute | solution.py:10
  307.9 5.4 copy-start.3
  308.1 15.3 %collective-permute-start.15 = (bf16[384,512]{1,0:T(8,128)(2,1)S(1)}, bf16[384,512]{1,0:T(8,128)(2,1)S(1)}, u32[]{:S(2)}, u32[]{:S(2)}) collective-permute-start(bf16[384,512]{1,0:T(8,128)(2,1)S(1)} %get-tuple-element.20), channel_id=1, source_target_pairs={{0,8},{1,9},{2,10},{3,11},{4,12},{5,13},{6,14},{7,15},{8,0},{9,1},... | collective-permute-start | bytes 1179656 | tf_op jit(solution)/shard_map/ppermute | solution.py:10
  308.7 14.7 %collective-permute-start.14 = (bf16[384,512]{1,0:T(8,128)(2,1)S(1)}, bf16[384,512]{1,0:T(8,128)(2,1)S(1)}, u32[]{:S(2)}, u32[]{:S(2)}) collective-permute-start(bf16[384,512]{1,0:T(8,128)(2,1)S(1)} %get-tuple-element.21), channel_id=1, source_target_pairs={{0,4},{1,5},{2,6},{3,7},{4,0},{5,1},{6,2},{7,3},{8,12},{9,13},{10,... | collective-permute-start | bytes 1179656 | tf_op jit(solution)/shard_map/ppermute | solution.py:10
  311.9 18.2 %collective-permute-start.13 = (bf16[384,512]{1,0:T(8,128)(2,1)S(1)}, bf16[384,512]{1,0:T(8,128)(2,1)S(1)}, u32[]{:S(2)}, u32[]{:S(2)}) collective-permute-start(bf16[384,512]{1,0:T(8,128)(2,1)S(1)} %get-tuple-element.22), channel_id=1, source_target_pairs={{0,2},{1,3},{2,0},{3,1},{4,6},{5,7},{6,4},{7,5},{8,10},{9,11},{10,... | collective-permute-start | bytes 1179656 | tf_op jit(solution)/shard_map/ppermute | solution.py:10
  313.2 16.9 %collective-permute-start.12 = (bf16[384,512]{1,0:T(8,128)(2,1)S(1)}, bf16[384,512]{1,0:T(8,128)(2,1)S(1)}, u32[]{:S(2)}, u32[]{:S(2)}) collective-permute-start(bf16[384,512]{1,0:T(8,128)(2,1)S(1)} %get-tuple-element.23), channel_id=1, source_target_pairs={{0,1},{1,0},{2,3},{3,2},{4,5},{5,4},{6,7},{7,6},{8,9},{9,8},{10,11... | collective-permute-start | bytes 1179656 | tf_op jit(solution)/shard_map/ppermute | solution.py:10
Sparse Core Ops, SparseCore 0:
  9.8 178.6 all-gather.1
  257.7 183.0 reduce-scatter.2
  443.3 96.0 reduce-scatter.4
